TPU v7x, 32 devices: a whole 2x2x4 slice. The times are simulated.
32 devices in a mesh: req: 8 (over z, y), tp: 4 (over x, core).
Axes of the slice: x: 2, y: 2, z: 4, core: 2. Of those that a mesh axis runs over, the one named last changes fastest.
Arguments:
- tokens_in: bfloat16 [24, 4, 2048], P('req'), may hold values from -6 to 6
- attn_norm: bfloat16 [2048], replicated, may hold values from 0.099609375 to 1.8984375
- qkv_weight: bfloat16 [2048, 3, 2048], P(None, None, 'tp'), may hold values from -0.125 to 0.125
- qkv_bias: bfloat16 [3, 2048], P(None, 'tp'), may hold values from -12 to 12
- out_weight: bfloat16 [2048, 2048], P('tp'), may hold values from -0.125 to 0.125
- cache_keys: bfloat16 [320, 128, 2048], P('req', None, 'tp'), may hold values from -12 to 12
- cache_values: bfloat16 [320, 128, 2048], P('req', None, 'tp'), may hold values from -6 to 6
- page_table: int32 [24, 37], replicated, may hold values from -1 to 319, as said below
- cache_lengths: int32 [24], replicated, may hold values from 1 to 4736, as said below
- mlp_norm: bfloat16 [2048], replicated, may hold values from 0.099609375 to 1.8984375
- routes: int32 [24, 4, 4], P('req'), may hold values from 0 to 7, all different within a row; in each aligned block of 12 rows (0 to 11, 12 to 23, ..., all dimensions but the last counted through in order) at most 6 rows name the same one
- route_gates: float32 [24, 4, 4], P('req'), may hold values from 0.05 to 0.5
- expert_w_gate: bfloat16 [8, 2048, 1408], P('req', None, 'tp'), may hold values from -0.125 to 0.125
- expert_w_up: bfloat16 [8, 2048, 1408], P('req', None, 'tp'), may hold values from -0.125 to 0.125
- expert_w_down: bfloat16 [8, 1408, 2048], P('req', 'tp'), may hold values from -0.15625 to 0.15625
- shared_w_gate: bfloat16 [2048, 5632], P('tp', 'req'), may hold values from -0.125 to 0.125
- shared_w_up: bfloat16 [2048, 5632], P('tp', 'req'), may hold values from -0.125 to 0.125
- shared_w_down: bfloat16 [5632, 2048], P('req', 'tp'), may hold values from -0.078125 to 0.078125
- shared_switch: bfloat16 [2048], replicated, may hold values from -0.125 to 0.125
Outputs:
- layer_out: bfloat16 [24, 4, 2048], P('req', None, 'tp')
Inputs may be any that keep to these rules, and one draw needn't show every extreme that they name: `page_table`: entry [r, j] is the pool page holding positions j*128 to (j+1)*128 - 1 of request r's cache, or -1. No pool page is named twice. 6 requests, drawn from the seed, have all 37 entries set, all outside the first 12 pages of every block of 40 pool pages; every other request r has exactly its first 4 entries set, all among pool pages (r // 3)*40 to (r // 3)*40 + 3*4 - 1. `cache_lengths`: A long request has 2368 to 4736 cached tokens, any other 1 to 512; both largest values occur in every draw. `routes`: the 4 experts of a token differ. Among the 12 tokens of each aligned block of rows (those of one index of req) no expert is named more than 6 times, and in some of those blocks one expert is named exactly 6 times.
All inputs are finite; a program needn't handle non-finite values.
Results may differ from a plain program's by a relative error of at most 0.006.
Values may be sent and summed in bfloat16 or wider, within the bound.
No kernel may reach another device: no remote copies, remote signals or barrier semaphores. Data moves between devices by JAX's collectives and lax.ppermute only.
A program may use at most 128 MiB of HBM per device.

v0:
```python
import math
import jax
import jax.numpy as jnp
from jax import lax
from jax.sharding import PartitionSpec as P

HD = 128
TOPK = 4
NEG = -1e30
EPS = 1e-06
THETA = 1000000.0
HIGHEST = lax.Precision.HIGHEST


def rms_norm(inputs, gain_vector):
    values = inputs.astype(jnp.float32)
    scaled = values * lax.rsqrt(jnp.mean(values * values, axis=-1, keepdims=True) + EPS)
    return (scaled * gain_vector.astype(jnp.float32)).astype(jnp.bfloat16)


def rotate(values, positions):
    half_dim = values.shape[-1] // 2
    exponents = jnp.arange(half_dim, dtype=jnp.float32) * (2.0 / values.shape[-1])
    frequency = jnp.power(THETA, -exponents)
    angles = positions.astype(jnp.float32)[..., None, None] * frequency
    cosines = jnp.cos(angles)
    sine_part = jnp.sin(angles)
    front_half = values[..., :half_dim]
    back_half = values[..., half_dim:]
    return jnp.concatenate(
        [
            front_half * cosines - back_half * sine_part,
            back_half * cosines + front_half * sine_part,
        ],
        axis=-1,
    )


def bcast_a2a(values, axis, count):
    spread = jnp.broadcast_to(values[None], (count,) + values.shape)
    return lax.all_to_all(spread, axis, 0, 0, tiled=True).reshape(
        (count * values.shape[0],) + values.shape[1:]
    )


def per_device(
    tokens_in,
    attn_norm,
    qkv_weight,
    qkv_bias,
    out_weight,
    cache_keys,
    cache_values,
    page_table,
    cache_lengths,
    mlp_norm,
    routes,
    route_gates,
    expert_w_gate,
    expert_w_up,
    expert_w_down,
    shared_w_gate,
    shared_w_up,
    shared_w_down,
    shared_switch,
):
    req_rows, step_count, model_width = tokens_in.shape
    head_width = qkv_weight.shape[2]
    local_heads = head_width // HD
    req_count = lax.axis_size("req")
    tp_count = lax.axis_size("tp")
    req_index = lax.axis_index("req")
    tp_index = lax.axis_index("tp")
    all_requests = page_table.shape[0]
    pool_here = cache_keys.shape[0]
    page_len = cache_keys.shape[1]
    score_scale = 1.0 / math.sqrt(HD)
    col_share = model_width // tp_count
    row_count = req_rows * step_count
    normed = rms_norm(tokens_in, attn_norm)
    projected = jnp.einsum(
        "rsd,dcf->rscf", normed, qkv_weight, preferred_element_type=jnp.float32
    ) + qkv_bias.astype(jnp.float32)
    own_lengths = lax.dynamic_slice_in_dim(cache_lengths, req_index * req_rows, req_rows)
    positions = own_lengths[:, None] + jnp.arange(step_count, dtype=jnp.int32)[None, :]
    head_shape = (req_rows, step_count, local_heads, HD)
    query_new = rotate(projected[:, :, 0].reshape(head_shape), positions).astype(jnp.bfloat16)
    key_new = rotate(projected[:, :, 1].reshape(head_shape), positions).astype(jnp.bfloat16)
    value_new = projected[:, :, 2].reshape(head_shape).astype(jnp.bfloat16)
    query_all = bcast_a2a(query_new, "req", req_count)
    slot_ids = req_index * pool_here + jnp.arange(pool_here, dtype=jnp.int32)
    matches = (page_table[:, :, None] == slot_ids[None, None, :]).astype(jnp.int32)
    request_ids = jnp.arange(all_requests, dtype=jnp.int32)
    page_ids = jnp.arange(page_table.shape[1], dtype=jnp.int32)
    owner = jnp.sum(matches * request_ids[:, None, None], axis=(0, 1))
    logical = jnp.sum(matches * page_ids[None, :, None], axis=(0, 1))
    present = jnp.sum(matches, axis=(0, 1)) > 0
    token_pos = logical[:, None] * page_len + jnp.arange(page_len, dtype=jnp.int32)[None, :]
    live = present[:, None] & (token_pos < cache_lengths[owner][:, None])
    page_queries = query_all[owner]
    page_keys = cache_keys.reshape(pool_here, page_len, local_heads, HD)
    page_values = cache_values.reshape(pool_here, page_len, local_heads, HD)
    scores = (
        jnp.einsum("pshd,pkhd->pshk", page_queries, page_keys, preferred_element_type=jnp.float32)
        * score_scale
    )
    page_mask = live[:, None, None, :]
    masked = jnp.where(page_mask, scores, NEG)
    page_max = jnp.max(masked, axis=-1)
    weights = jnp.where(page_mask, jnp.exp(masked - page_max[..., None]), 0.0)
    page_sum = jnp.sum(weights, axis=-1)
    page_out = jnp.einsum(
        "pshk,pkhd->pshd",
        weights.astype(jnp.bfloat16),
        page_values,
        preferred_element_type=jnp.float32,
    )
    belongs = (owner[None, :] == request_ids[:, None]) & present[None, :]
    owned = belongs[:, :, None, None]
    local_max = jnp.max(jnp.where(owned, page_max[None], NEG), axis=1)
    factors = jnp.where(owned, jnp.exp(page_max[None] - local_max[:, None]), 0.0)
    local_out = jnp.einsum("rpsh,pshd->rshd", factors, page_out, precision=HIGHEST)
    local_sum = jnp.einsum("rpsh,psh->rsh", factors, page_sum, precision=HIGHEST)
    stat_width = step_count * local_heads
    stat_row = jnp.concatenate(
        [
            local_max.reshape(all_requests, stat_width),
            local_sum.reshape(all_requests, stat_width),
            jnp.zeros((all_requests, HD - 2 * stat_width), jnp.float32),
        ],
        axis=1,
    )
    packed = jnp.concatenate(
        [local_out.reshape(all_requests, stat_width, HD), stat_row[:, None, :]], axis=1
    )
    gathered = lax.all_to_all(packed, "req", 0, 0, tiled=True).reshape(
        req_count, req_rows, stat_width + 1, HD
    )
    part_out = gathered[:, :, :stat_width, :]
    part_max = gathered[:, :, stat_width, :stat_width]
    part_sum = gathered[:, :, stat_width, stat_width : 2 * stat_width]
    cache_max = jnp.max(part_max, axis=0)
    rescale = jnp.exp(part_max - cache_max[None])
    cache_out = jnp.sum(part_out * rescale[..., None], axis=0).reshape(
        req_rows, step_count, local_heads, HD
    )
    cache_sum = jnp.sum(part_sum * rescale, axis=0).reshape(req_rows, step_count, local_heads)
    cache_max = cache_max.reshape(req_rows, step_count, local_heads)
    new_scores = (
        jnp.einsum("rshd,rthd->rsht", query_new, key_new, preferred_element_type=jnp.float32)
        * score_scale
    )
    causal = jnp.arange(step_count)[:, None] >= jnp.arange(step_count)[None, :]
    new_mask = causal[None, :, None, :]
    new_masked = jnp.where(new_mask, new_scores, NEG)
    new_max = jnp.max(new_masked, axis=-1)
    new_weights = jnp.where(new_mask, jnp.exp(new_masked - new_max[..., None]), 0.0)
    new_sum = jnp.sum(new_weights, axis=-1)
    new_out = jnp.einsum(
        "rsht,rthd->rshd",
        new_weights.astype(jnp.bfloat16),
        value_new,
        preferred_element_type=jnp.float32,
    )
    top_max = jnp.maximum(cache_max, new_max)
    cache_factor = jnp.exp(cache_max - top_max)
    new_factor = jnp.exp(new_max - top_max)
    attended = (cache_out * cache_factor[..., None] + new_out * new_factor[..., None]) / (
        cache_sum * cache_factor + new_sum * new_factor
    )[..., None]
    attended = attended.astype(jnp.bfloat16).reshape(row_count, head_width)
    attn_part = jnp.dot(attended, out_weight, preferred_element_type=jnp.float32)
    attn_full = jnp.sum(
        bcast_a2a(attn_part, "tp", tp_count).reshape(tp_count, row_count, model_width), axis=0
    )
    resid = tokens_in.reshape(row_count, model_width).astype(jnp.float32) + attn_full
    mixed = rms_norm(resid, mlp_norm)
    expert_count = req_count * expert_w_gate.shape[0]
    capacity = max(2, (row_count * TOPK + expert_count - 1) // expert_count)
    picks = routes.reshape(row_count * TOPK)
    gates_flat = route_gates.reshape(row_count * TOPK)
    expert_hot = (picks[:, None] == jnp.arange(expert_count, dtype=jnp.int32)[None, :]).astype(
        jnp.int32
    )
    slot_index = jnp.sum((jnp.cumsum(expert_hot, axis=0) - 1) * expert_hot, axis=1)
    destination = picks * capacity + slot_index
    dest_hot = (
        destination[:, None] == jnp.arange(expert_count * capacity, dtype=jnp.int32)[None, :]
    ).astype(jnp.float32)
    token_hot = (
        (jnp.arange(row_count * TOPK, dtype=jnp.int32) // TOPK)[:, None]
        == jnp.arange(row_count, dtype=jnp.int32)[None, :]
    ).astype(jnp.float32)
    placement = jnp.einsum("cx,ct->xt", dest_hot, token_hot, precision=HIGHEST).astype(jnp.bfloat16)
    outgoing = jnp.dot(placement, mixed, preferred_element_type=jnp.float32).astype(jnp.bfloat16)
    combine_map = jnp.einsum(
        "ct,cx->tx", token_hot, dest_hot * gates_flat[:, None], precision=HIGHEST
    )
    w_gate_here = expert_w_gate[0]
    w_up_here = expert_w_up[0]
    w_down_here = expert_w_down[0]
    mixed_cols = lax.dynamic_slice_in_dim(mixed, tp_index * col_share, col_share, 1)
    shared_send = jnp.broadcast_to(mixed_cols[None], (req_count, row_count, col_share))
    dispatch = jnp.concatenate(
        [
            outgoing.reshape(req_count, capacity * model_width),
            shared_send.reshape(req_count, row_count * col_share),
        ],
        axis=1,
    )
    received = lax.all_to_all(dispatch, "req", 0, 0, tiled=True)
    item_count = capacity
    flat_rows = received[:, : capacity * model_width].reshape(req_count * capacity, model_width)
    piece = received[:, capacity * model_width :].reshape(req_count * row_count, col_share)
    gate_pre = jnp.dot(flat_rows, w_gate_here, preferred_element_type=jnp.float32)
    up_pre = jnp.dot(flat_rows, w_up_here, preferred_element_type=jnp.float32)
    hidden = (jax.nn.silu(gate_pre) * up_pre).astype(jnp.bfloat16)
    partial_out = jnp.dot(hidden, w_down_here, preferred_element_type=jnp.float32)
    expert_rows = req_count * capacity
    partial_split = partial_out.reshape(expert_rows, tp_count, col_share).transpose(1, 0, 2)
    gate_part = jnp.dot(piece, shared_w_gate, preferred_element_type=jnp.float32)
    up_part = jnp.dot(piece, shared_w_up, preferred_element_type=jnp.float32)
    unit_count = shared_w_gate.shape[1]
    all_rows = req_count * row_count
    expert_high = partial_split.astype(jnp.bfloat16)
    expert_low = (partial_split - expert_high.astype(jnp.float32)).astype(jnp.bfloat16)
    shared_pre = jnp.concatenate([gate_part, up_part], axis=1).astype(jnp.bfloat16)
    reduce_in = jnp.concatenate(
        [
            expert_high.reshape(tp_count, expert_rows * col_share),
            expert_low.reshape(tp_count, expert_rows * col_share),
            jnp.broadcast_to(
                shared_pre.reshape(1, all_rows * 2 * unit_count),
                (tp_count, all_rows * 2 * unit_count),
            ),
        ],
        axis=1,
    )
    reduce_out = lax.all_to_all(reduce_in, "tp", 0, 0, tiled=True).astype(jnp.float32)
    expert_part = expert_rows * col_share
    expert_sum = jnp.sum(
        reduce_out[:, :expert_part] + reduce_out[:, expert_part : 2 * expert_part], axis=0
    ).reshape(expert_rows, col_share)
    shared_sum = jnp.sum(reduce_out[:, 2 * expert_part :], axis=0).reshape(all_rows, 2 * unit_count)
    hidden_all = (jax.nn.silu(shared_sum[:, :unit_count]) * shared_sum[:, unit_count:]).astype(
        jnp.bfloat16
    )
    shared_down = jnp.dot(hidden_all, shared_w_down, preferred_element_type=jnp.float32)
    ey = expert_sum.astype(jnp.bfloat16).astype(jnp.float32)
    back_in = jnp.concatenate(
        [
            ey.reshape(req_count, capacity * col_share),
            shared_down.reshape(req_count, row_count * col_share),
        ],
        axis=1,
    )
    back = lax.all_to_all(back_in, "req", 0, 0, tiled=True)
    returned = back[:, : capacity * col_share].reshape(expert_count * capacity, col_share)
    shared_mine = jnp.sum(
        back[:, capacity * col_share :].reshape(req_count, row_count, col_share), axis=0
    )
    moe_out = jnp.dot(combine_map, returned, precision=HIGHEST)
    switch = jax.nn.sigmoid(jnp.dot(mixed, shared_switch, preferred_element_type=jnp.float32))
    resid_mine = lax.dynamic_slice_in_dim(resid, tp_index * col_share, col_share, 1)
    final = resid_mine + moe_out + switch[:, None] * shared_mine
    return final.astype(jnp.bfloat16).reshape(req_rows, step_count, col_share)


def solution(mesh):
    return jax.shard_map(
        per_device,
        mesh=mesh,
        in_specs=(
            P("req", None, None),
            P(),
            P(None, None, "tp"),
            P(None, "tp"),
            P("tp", None),
            P("req", None, "tp"),
            P("req", None, "tp"),
            P(),
            P(),
            P(),
            P("req", None, None),
            P("req", None, None),
            P("req", None, "tp"),
            P("req", None, "tp"),
            P("req", "tp", None),
            P("tp", "req"),
            P("tp", "req"),
            P("req", "tp"),
            P(),
        ),
        out_specs=P("req", None, "tp"),
        check_vma=False,
    )
```

profile of v0, /device:TPU:0, one launch (start us, length us, event | category | flops | bytes accessed | tf_op | source)
XLA Modules:
  0.0 155.8 jit_solution(10692810095028306036)
XLA Ops:
  3.3 3.8 %fusion.30 = f32[3,4,3,512]{3,1,2,0:T(4,128)S(1)} fusion(bf16[2048,3,512]{2,0,1:T(8,128)(2,1)} %param.21, bf16[3,4,2048]{2,1,0:T(4,128)(2,1)} %param.19, f32[2048]{0:T(1024)S(1)} %convert_element_type.114, f32[3,4]{1,0:T(4,128)S(1)} %add_rsqrt_fusion.1, f32[3,512]{1,0:T(4,128)S(1)} %convert_element_type.116), kind=kOutput, calls=%fused_computation.28 | convolution fusion | flops 75614208 | bytes 6428720 | tf_op jit(solution)/shard_map/rsd,dcf->rscf/dot_general | solution.py:81
  8.1 7.3 %all-to-all-start = ((bf16[8,3,4,4,128]{4,3,2,1,0:T(4,128)(2,1)}), bf16[8,3,4,4,128]{4,3,2,1,0:T(4,128)(2,1)S(1)}, u32[]{:S(2)}, u32[]{:S(2)}) async-start(bf16[8,3,4,4,128]{4,3,2,1,0:T(4,128)(2,1)} %broadcast_in_dim.81), calls=%async_computation | async-start | bytes 196608 | tf_op jit(solution)/shard_map/all_to_all | solution.py:41
  17.2 5.3 %all-to-all-done = bf16[8,3,4,4,128]{4,3,2,1,0:T(4,128)(2,1)S(1)} async-done(((bf16[8,3,4,4,128]{4,3,2,1,0:T(4,128)(2,1)}), bf16[8,3,4,4,128]{4,3,2,1,0:T(4,128)(2,1)S(1)}, u32[]{:S(2)}, u32[]{:S(2)}) %all-to-all-start) | async-done | bytes 98336 | tf_op jit(solution)/shard_map/all_to_all | solution.py:41
  23.2 5.4 %fusion.134 = (f32[40,4,4]{1,2,0:T(4,128)S(1)}, f32[40,4,4,128]{3,1,2,0:T(4,128)S(1)}) fusion(bf16[40,4,4,128]{3,2,1,0:T(4,128)(2,1)S(1)} %gather_fusion.1, pred[40,128]{1,0:T(8,128)(4,1)S(1)} %fusion.97, bf16[40,128,512]{2,1,0:T(8,128)(2,1)} %param.24), kind=kOutput, calls=%fused_computation.184 | convolution fusion | flops 21216640 | bytes 5742080 | tf_op jit(solution)/shard_map/pshd,pkhd->pshk/dot_general | solution.py:104
  29.5 4.0 %fusion.18 = f32[40,4,4,128]{3,1,2,0:T(4,128)S(1)} fusion(f32[40,4,4,128]{3,1,2,0:T(4,128)S(1)} %get-tuple-element.31, f32[40,4,4]{1,2,0:T(4,128)S(1)} %get-tuple-element.30, pred[40,128]{1,0:T(8,128)(4,1)S(1)} %fusion.97, bf16[40,128,512]{2,1,0:T(8,128)(2,1)} %param.25), kind=kOutput, calls=%fused_computation.22 | convolution fusion | flops 21217280 | bytes 5905920 | tf_op jit(solution)/shard_map/pshk,pkhd->pshd/dot_general | solution.py:112
  35.7 3.4 %all-to-all-start.1 = ((f32[24,17,128]{2,1,0:T(8,128)}), f32[24,17,128]{2,1,0:T(8,128)S(1)}, u32[]{:S(2)}, u32[]{:S(2)}) async-start(f32[24,17,128]{2,1,0:T(8,128)} %pad_maximum_fusion), calls=%async_computation.1 | async-start | bytes 589824 | tf_op jit(solution)/shard_map/all_to_all | solution.py:136
  39.4 8.3 %all-to-all-done.1 = f32[24,17,128]{2,1,0:T(8,128)S(1)} async-done(((f32[24,17,128]{2,1,0:T(8,128)}), f32[24,17,128]{2,1,0:T(8,128)S(1)}, u32[]{:S(2)}, u32[]{:S(2)}) %all-to-all-start.1) | async-done | bytes 208928 | tf_op jit(solution)/shard_map/all_to_all | solution.py:136
  50.0 3.5 %all-to-all-start.2 = ((f32[4,12,2048]{2,1,0:T(8,128)}), f32[4,12,2048]{2,1,0:T(8,128)S(1)}, u32[]{:S(2)}, u32[]{:S(2)}) async-start(f32[4,12,2048]{2,1,0:T(8,128)} %broadcast_in_dim.92), calls=%async_computation.2 | async-start | bytes 1048576 | tf_op jit(solution)/shard_map/all_to_all | solution.py:41
  53.8 8.5 %all-to-all-done.2 = f32[4,12,2048]{2,1,0:T(8,128)S(1)} async-done(((f32[4,12,2048]{2,1,0:T(8,128)}), f32[4,12,2048]{2,1,0:T(8,128)S(1)}, u32[]{:S(2)}, u32[]{:S(2)}) %all-to-all-start.2) | async-done | bytes 393248 | tf_op jit(solution)/shard_map/all_to_all | solution.py:41
  64.9 13.5 %all_to_all.48 = bf16[8,2,9216]{2,1,0:T(2,128)(2,1)S(1)} all-to-all(bf16[8,2,9216]{2,1,0:T(2,128)(2,1)S(1)} %reshape.410), channel_id=1, replica_groups=mesh['req'=8,'tp'=4] {'req'}, dimensions={0} | all-to-all | bytes 589824 | tf_op jit(solution)/shard_map/all_to_all | solution.py:211
  79.3 1.9 %fusion.13 = f32[48,352]{1,0:T(8,128)S(1)} fusion(bf16[48,2048]{1,0:T(8,128)(2,1)S(1)} %reshape.374, bf16[1,2048,352]{1,2,0:T(8,128)(2,1)} %param.31), kind=kOutput, calls=%fused_computation.19 | convolution fusion | flops 69206016 | bytes 1705984 | tf_op jit(solution)/shard_map/dot_general | solution.py:215
  81.2 2.9 %convert_bitcast_fusion = (bf16[1,4,48,512]{3,2,1,0:T(8,128)(2,1)S(1)}, bf16[1,4,48,512]{3,2,1,0:T(8,128)(2,1)S(1)}) fusion(bf16[44,4,8,512]{3,2,1,0:T(8,128)(2,1)} %bitcast.183, bf16[48,2048]{1,0:T(8,128)(2,1)S(1)} %reshape.374, bf16[1,2048,352]{1,2,0:T(8,128)(2,1)} %param.32, f32[48,352]{1,0:T(8,128)S(1)} %fusion.13), kind=kOutput, calls=%fused_computation.85 | convolution fusion | flops 138906624 | bytes 3540992 | tf_op jit(solution)/shard_map/dot_general | solution.py:218
  84.3 1.5 convolution_convert_fusion.1
  85.8 1.5 convolution_convert_fusion.2
  87.9 5.0 %maximum_bitcast_fusion = bf16[4,1,184320]{2,0,1:T(4,128)(2,1)} fusion(bf16[4,24576]{1,0:T(4,128)(2,1)S(1)} %bitcast.191, bf16[4,24576]{1,0:T(4,128)(2,1)S(1)} %bitcast.190, bf16[184320]{0:T(1024)(128)(2,1)S(1)} %pad.4.clone), kind=kLoop, calls=%fused_computation.13 | loop fusion | flops 4423680 | bytes 2236416 | tf_op jit(solution)/shard_map/all_to_all | solution.py:239
  92.9 4.7 %reduce.4 = bf16[4,184320]{1,0:T(4,128)(2,1)} reduce(bf16[4,1,184320]{2,0,1:T(4,128)(2,1)} %maximum_bitcast_fusion, bf16[]{:T(256)} %broadcast.288), dimensions={1}, to_apply=%copy.166.reduce_sub_computation | reduce | bytes 2949122 | tf_op jit(solution)/shard_map/all_to_all | solution.py:239
  97.6 4.0 %reshape.412 = bf16[4,2,92160]{2,1,0:T(2,128)(2,1)} reshape(bf16[4,184320]{1,0:T(4,128)(2,1)} %reduce.4) | data formatting | bytes 2949120
  101.6 23.4 %all_to_all.49 = bf16[4,2,92160]{2,1,0:T(2,128)(2,1)} all-to-all(bf16[4,2,92160]{2,1,0:T(2,128)(2,1)} %reshape.412), channel_id=1, replica_groups=mesh['req'=8,'tp'=4] {'tp'}, dimensions={0} | all-to-all | bytes 2949120 | tf_op jit(solution)/shard_map/all_to_all | solution.py:239
  125.0 4.4 %reshape.413 = bf16[4,1,184320]{2,1,0:T(2,128)(2,1)} reshape(bf16[4,2,92160]{2,1,0:T(2,128)(2,1)} %all_to_all.49) | data formatting | bytes 2949120
  129.4 3.7 %copy.242 = f32[4,1,184320]{2,0,1:T(4,128)S(1)} copy(bf16[4,1,184320]{2,1,0:T(2,128)(2,1)} %reshape.413) | data formatting | bytes 4423680
  133.4 5.6 %slice_reduce_fusion = f32[135168]{0:T(1024)S(1)} fusion(f32[4,184320]{1,0:T(4,128)S(1)} %bitcast.182), kind=kLoop, calls=%fused_computation.12 | loop fusion | flops 405504 | bytes 2703360 | tf_op jit(solution)/shard_map/reduce_sum | solution.py:244
  139.1 1.4 fusion.73
  141.6 3.4 %all-to-all-start.5 = ((f32[8,1,9216]{2,1,0:T(1,128)}), f32[8,1,9216]{2,1,0:T(1,128)S(1)}, u32[]{:S(2)}, u32[]{:S(2)}) async-start(f32[8,1,9216]{2,1,0:T(1,128)} %all_to_all.39), calls=%async_computation.5 | async-start | bytes 589824 | tf_op jit(solution)/shard_map/all_to_all | solution.py:257
  145.5 9.3 %all-to-all-done.5 = f32[8,1,9216]{2,1,0:T(1,128)S(1)} async-done(((f32[8,1,9216]{2,1,0:T(1,128)}), f32[8,1,9216]{2,1,0:T(1,128)S(1)}, u32[]{:S(2)}, u32[]{:S(2)}) %all-to-all-start.5) | async-done | bytes 294944 | tf_op jit(solution)/shard_map/all_to_all | solution.py:257
  (123 shorter events, 19.5 us)
Async XLA Ops:
  0.0 48.8 %copy-start = (bf16[512,2048]{1,0:T(8,128)(2,1)S(1)}, bf16[512,2048]{1,0:T(8,128)(2,1)}, u32[]{:S(2)}) copy-start(bf16[512,2048]{1,0:T(8,128)(2,1)} %param.23) | copy-start | bytes 6291460
  3.3 12.1 %copy-start.4 = (s32[3,4,4]{2,1,0:T(4,128)S(1)}, s32[3,4,4]{2,1,0:T(4,128)}, u32[]{:S(2)}) copy-start(s32[3,4,4]{2,1,0:T(4,128)} %param.29) | copy-start | bytes 580
  3.3 12.2 %copy-start.3 = (s32[24,37]{1,0:T(8,128)S(1)}, s32[24,37]{1,0:T(8,128)}, u32[]{:S(2)}) copy-start(s32[24,37]{1,0:T(8,128)} %param.26) | copy-start | bytes 10660
  3.3 12.6 %copy-start.1 = (s32[24]{0:T(128)S(1)}, s32[24]{0:T(128)}, u32[]{:S(2)}) copy-start(s32[24]{0:T(128)} %param.27) | copy-start | bytes 292
  8.1 14.4 %all-to-all-start = ((bf16[8,3,4,4,128]{4,3,2,1,0:T(4,128)(2,1)}), bf16[8,3,4,4,128]{4,3,2,1,0:T(4,128)(2,1)S(1)}, u32[]{:S(2)}, u32[]{:S(2)}) async-start(bf16[8,3,4,4,128]{4,3,2,1,0:T(4,128)(2,1)} %broadcast_in_dim.81), calls=%async_computation | async-start | bytes 196608 | tf_op jit(solution)/shard_map/all_to_all | solution.py:41
  35.7 12.0 %all-to-all-start.1 = ((f32[24,17,128]{2,1,0:T(8,128)}), f32[24,17,128]{2,1,0:T(8,128)S(1)}, u32[]{:S(2)}, u32[]{:S(2)}) async-start(f32[24,17,128]{2,1,0:T(8,128)} %pad_maximum_fusion), calls=%async_computation.1 | async-start | bytes 589824 | tf_op jit(solution)/shard_map/all_to_all | solution.py:136
  39.1 14.4 %copy-start.2 = (bf16[3,4,2048]{2,1,0:T(4,128)(2,1)S(1)}, bf16[3,4,2048]{2,1,0:T(4,128)(2,1)}, u32[]{:S(2)}) copy-start(bf16[3,4,2048]{2,1,0:T(4,128)(2,1)} %param.19) | copy-start | bytes 147460
  39.3 14.2 %copy-start.6 = (bf16[2048]{0:T(1024)(128)(2,1)S(1)}, bf16[2048]{0:T(1024)(128)(2,1)}, u32[]{:S(2)}) copy-start(bf16[2048]{0:T(1024)(128)(2,1)} %param.28) | copy-start | bytes 12292
  50.0 12.3 %all-to-all-start.2 = ((f32[4,12,2048]{2,1,0:T(8,128)}), f32[4,12,2048]{2,1,0:T(8,128)S(1)}, u32[]{:S(2)}, u32[]{:S(2)}) async-start(f32[4,12,2048]{2,1,0:T(8,128)} %broadcast_in_dim.92), calls=%async_computation.2 | async-start | bytes 1048576 | tf_op jit(solution)/shard_map/all_to_all | solution.py:41
  138.9 6.1 %copy-start.5 = (f32[3,4,4]{2,1,0:T(4,128)S(1)}, f32[3,4,4]{2,1,0:T(4,128)}, u32[]{:S(2)}) copy-start(f32[3,4,4]{2,1,0:T(4,128)} %param.30) | copy-start | bytes 580
  138.9 6.1 %copy-start.7 = (bf16[2048]{0:T(1024)(128)(2,1)S(1)}, bf16[2048]{0:T(1024)(128)(2,1)}, u32[]{:S(2)}) copy-start(bf16[2048]{0:T(1024)(128)(2,1)} %param.37) | copy-start | bytes 12292
  141.6 13.3 %all-to-all-start.5 = ((f32[8,1,9216]{2,1,0:T(1,128)}), f32[8,1,9216]{2,1,0:T(1,128)S(1)}, u32[]{:S(2)}, u32[]{:S(2)}) async-start(f32[8,1,9216]{2,1,0:T(1,128)} %all_to_all.39), calls=%async_computation.5 | async-start | bytes 589824 | tf_op jit(solution)/shard_map/all_to_all | solution.py:257
where the time goes:
time: 157 us; the launch traced here: 156 us
  blocking collectives  36.9 us (24%)
  waiting for transfers between devices  31.4 us (20%)
  matrix products  25.4 us (16%)
  other arithmetic  22.2 us (14%)
  local copies, waits for them, and re-layouts  21.7 us (14%)
  starting transfers between devices  17.6 us (11%)
    all_to_all x1, blocking collectives, per_device(): lax.all_to_all(reduce_in, 'tp', 0, 0, tiled=True).astype(jnp.float32)  23.4 us
    all_to_all x2, waiting for transfers between devices, bcast_a2a(): lax.all_to_all(spread, axis, 0, 0, tiled=True)  13.8 us
    all_to_all x1, blocking collectives, per_device(): received = lax.all_to_all(dispatch, 'req', 0, 0, tiled=True)  13.5 us
    unnamed x29, local copies, waits for them, and re-layouts  13.2 us
    all_to_all x2, starting transfers between devices, bcast_a2a(): lax.all_to_all(spread, axis, 0, 0, tiled=True)  10.8 us
    all_to_all x2, other arithmetic, per_device(): lax.all_to_all(reduce_in, 'tp', 0, 0, tiled=True).astype(jnp.float32)  9.7 us
    all_to_all x1, waiting for transfers between devices, per_device(): back = lax.all_to_all(back_in, 'req', 0, 0, tiled=True)  9.34 us
    all_to_all x1, waiting for transfers between devices, per_device(): lax.all_to_all(packed, 'req', 0, 0, tiled=True)  8.27 us
  transfers between devices with their start and end apart: 4, of which 4 were waited for; matrix products, arithmetic and copies ran while one was open for 2% of the time, Pallas kernels for 0%

commit v1 on v0

--- a/solution.py
+++ b/solution.py
@@ -10,6 +10,22 @@
 EPS = 1e-06
 THETA = 1000000.0
 HIGHEST = lax.Precision.HIGHEST
+
+
+def lift_the_lots_all(view, row_dim, buf):
+    front, side_arr = (view.shape[:row_dim], view.shape[row_dim + 1 :])
+    before = view.reshape(*front, buf, -1, *side_arr)
+    main = jnp.moveaxis(before, row_dim, 0)
+    return main
+
+
+def compute_shifts_all_for(inner_x, in_dim):
+    inner_x = jnp.moveaxis(inner_x, 0, in_dim)
+    seen_now = inner_x.shape
+    built = inner_x.reshape(
+        *seen_now[:in_dim], seen_now[in_dim] * seen_now[in_dim + 1], *seen_now[in_dim + 2 :]
+    )
+    return built
 
 
 def rms_norm(inputs, gain_vector):
@@ -133,9 +149,28 @@
     packed = jnp.concatenate(
         [local_out.reshape(all_requests, stat_width, HD), stat_row[:, None, :]], axis=1
     )
-    gathered = lax.all_to_all(packed, "req", 0, 0, tiled=True).reshape(
-        req_count, req_rows, stat_width + 1, HD
-    )
+
+    def _map_hubs(vec, target, s0, axis_name):
+        x_new = lax.axis_index(axis_name)
+        spare = lax.axis_size(axis_name)
+        everything, field_out = (spare, x_new)
+        all_values = lift_the_lots_all(target, vec, everything)
+        parts_seen = [all_values[field_out]]
+        for k0 in range(1, everything):
+            item_now = all_values[field_out ^ k0]
+            parts_seen.append(
+                lax.ppermute(
+                    item_now,
+                    axis_name=axis_name,
+                    perm=[(dev_i, dev_i ^ k0) for dev_i in range(everything)],
+                )
+            )
+        newest = jnp.stack(parts_seen)
+        all_values = newest[field_out ^ jnp.arange(everything)]
+        kept_arr = compute_shifts_all_for(all_values, s0)
+        return kept_arr
+
+    gathered = _map_hubs(0, packed, 0, "req").reshape(req_count, req_rows, stat_width + 1, HD)
     part_out = gathered[:, :, :stat_width, :]
     part_max = gathered[:, :, stat_width, :stat_width]
     part_sum = gathered[:, :, stat_width, stat_width : 2 * stat_width]

time: 157 us -> 161 us (1.025)
  starting transfers between devices: 17.6 us -> 23.9 us
    ppermute x0 -> x7, starting transfers between devices: none -> 9.68 us  [_map_hubs(): lax.ppermute(item_now, axis_name=axis_name, perm=[(dev_i, dev_i ^ k0) for...]
    all_to_all x1 -> x0, waiting for transfers between devices: 8.27 us -> none  [per_device(): lax.all_to_all(packed, 'req', 0, 0, tiled=True)]
    ppermute x0 -> x7, waiting for transfers between devices: none -> 7.15 us  [_map_hubs(): lax.ppermute(item_now, axis_name=axis_name, perm=[(dev_i, dev_i ^ k0) for...]
    all_to_all x1 -> x0, starting transfers between devices: 3.42 us -> none  [per_device(): lax.all_to_all(packed, 'req', 0, 0, tiled=True)]
    unnamed x29 -> x36, local copies, waits for them, and re-layouts: 13.2 us -> 13.3 us
  transfers between devices with their start and end apart: 4 -> 10, of which waited for: 4 -> 5; matrix products, arithmetic and copies ran while one was open for 2% -> 2% of each run, Pallas kernels for 0% -> 0%
where the time goes in v1:
time: 161 us; the launch traced here: 160 us
  blocking collectives  36.7 us (23%)
  waiting for transfers between devices  30 us (19%)
  matrix products  24.9 us (15%)
  starting transfers between devices  23.9 us (15%)
  local copies, waits for them, and re-layouts  22.5 us (14%)
  other arithmetic  21.6 us (13%)
    all_to_all x1, blocking collectives, per_device(): lax.all_to_all(reduce_in, 'tp', 0, 0, tiled=True).astype(jnp.float32)  23.4 us
    all_to_all x2, waiting for transfers between devices, bcast_a2a(): lax.all_to_all(spread, axis, 0, 0, tiled=True)  13.5 us
    all_to_all x1, blocking collectives, per_device(): received = lax.all_to_all(dispatch, 'req', 0, 0, tiled=True)  13.3 us
    unnamed x36, local copies, waits for them, and re-layouts  13.3 us
    all_to_all x2, starting transfers between devices, bcast_a2a(): lax.all_to_all(spread, axis, 0, 0, tiled=True)  10.7 us
    all_to_all x2, other arithmetic, per_device(): lax.all_to_all(reduce_in, 'tp', 0, 0, tiled=True).astype(jnp.float32)  9.7 us
    ppermute x7, starting transfers between devices, _map_hubs(): lax.ppermute(item_now, axis_name=axis_name, perm=[(dev_i, dev_i ^ k0) for...  9.68 us
    all_to_all x1, waiting for transfers between devices, per_device(): back = lax.all_to_all(back_in, 'req', 0, 0, tiled=True)  9.34 us
  transfers between devices with their start and end apart: 10, of which 5 were waited for; matrix products, arithmetic and copies ran while one was open for 2% of the time, Pallas kernels for 0%

profile of v1, /device:TPU:0, one launch (start us, length us, event | category | flops | bytes accessed | tf_op | source)
XLA Modules:
  0.0 160.4 jit_solution(16037145637811731280)
XLA Ops:
  3.3 3.8 %fusion.30 = f32[3,4,3,512]{3,1,2,0:T(4,128)S(1)} fusion(bf16[2048,3,512]{2,0,1:T(8,128)(2,1)} %param.21, bf16[3,4,2048]{2,1,0:T(4,128)(2,1)} %param.19, f32[2048]{0:T(1024)S(1)} %convert_element_type.114, f32[3,4]{1,0:T(4,128)S(1)} %add_rsqrt_fusion.1, f32[3,512]{1,0:T(4,128)S(1)} %convert_element_type.116), kind=kOutput, calls=%fused_computation.30 | convolution fusion | flops 75614208 | bytes 6428720 | tf_op jit(solution)/shard_map/rsd,dcf->rscf/dot_general | solution.py:97
  8.1 7.3 %all-to-all-start = ((bf16[8,3,4,4,128]{4,3,2,1,0:T(4,128)(2,1)}), bf16[8,3,4,4,128]{4,3,2,1,0:T(4,128)(2,1)S(1)}, u32[]{:S(2)}, u32[]{:S(2)}) async-start(bf16[8,3,4,4,128]{4,3,2,1,0:T(4,128)(2,1)} %broadcast_in_dim.79), calls=%async_computation | async-start | bytes 196608 | tf_op jit(solution)/shard_map/all_to_all | solution.py:57
  17.5 5.0 %all-to-all-done = bf16[8,3,4,4,128]{4,3,2,1,0:T(4,128)(2,1)S(1)} async-done(((bf16[8,3,4,4,128]{4,3,2,1,0:T(4,128)(2,1)}), bf16[8,3,4,4,128]{4,3,2,1,0:T(4,128)(2,1)S(1)}, u32[]{:S(2)}, u32[]{:S(2)}) %all-to-all-start) | async-done | bytes 98336 | tf_op jit(solution)/shard_map/all_to_all | solution.py:57
  23.2 5.4 %fusion.127 = (f32[40,4,4]{1,2,0:T(4,128)S(1)}, f32[40,4,4,128]{3,1,2,0:T(4,128)S(1)}) fusion(bf16[40,4,4,128]{3,2,1,0:T(4,128)(2,1)S(1)} %gather_fusion.1, pred[40,128]{1,0:T(8,128)(4,1)S(1)} %fusion.91, bf16[40,128,512]{2,1,0:T(8,128)(2,1)} %param.24), kind=kOutput, calls=%fused_computation.195 | convolution fusion | flops 21216640 | bytes 5742080 | tf_op jit(solution)/shard_map/pshd,pkhd->pshk/dot_general | solution.py:120
  29.7 4.0 %fusion.18 = f32[40,4,4,128]{3,1,2,0:T(4,128)S(1)} fusion(f32[40,4,4,128]{3,1,2,0:T(4,128)S(1)} %get-tuple-element.39, f32[40,4,4]{1,2,0:T(4,128)S(1)} %get-tuple-element.38, pred[40,128]{1,0:T(8,128)(4,1)S(1)} %fusion.91, bf16[40,128,512]{2,1,0:T(8,128)(2,1)} %param.25), kind=kOutput, calls=%fused_computation.23 | convolution fusion | flops 21217280 | bytes 5905920 | tf_op jit(solution)/shard_map/pshk,pkhd->pshd/dot_general | solution.py:128
  35.4 1.7 %collective-permute-start.6 = (f32[3,17,128]{2,1,0:T(8,128)S(1)}, f32[3,17,128]{2,1,0:T(8,128)S(1)}, u32[]{:S(2)}, u32[]{:S(2)}) collective-permute-start(f32[3,17,128]{2,1,0:T(8,128)S(1)} %get-tuple-element.20), channel_id=1, source_target_pairs={{0,28},{4,24},{8,20},{12,16},{16,12},{20,8},{24,4},{28,0},{1,29},{... | collective-permute-start | bytes 78344 | tf_op jit(solution)/shard_map/ppermute | solution.py:162
  37.1 3.3 %collective-permute-start.5 = (f32[3,17,128]{2,1,0:T(8,128)S(1)}, f32[3,17,128]{2,1,0:T(8,128)S(1)}, u32[]{:S(2)}, u32[]{:S(2)}) collective-permute-start(f32[3,17,128]{2,1,0:T(8,128)S(1)} %get-tuple-element.21), channel_id=1, source_target_pairs={{0,24},{4,28},{8,16},{12,20},{16,8},{20,12},{24,0},{28,4},{1,25},{... | collective-permute-start | bytes 78344 | tf_op jit(solution)/shard_map/ppermute | solution.py:162
  40.4 2.7 %collective-permute-start.3 = (f32[3,17,128]{2,1,0:T(8,128)S(1)}, f32[3,17,128]{2,1,0:T(8,128)S(1)}, u32[]{:S(2)}, u32[]{:S(2)}) collective-permute-start(f32[3,17,128]{2,1,0:T(8,128)S(1)} %get-tuple-element.23), channel_id=1, source_target_pairs={{0,16},{4,20},{8,24},{12,28},{16,0},{20,4},{24,8},{28,12},{1,17},{... | collective-permute-start | bytes 78344 | tf_op jit(solution)/shard_map/ppermute | solution.py:162
  43.1 3.9 %collective-permute-done.1 = f32[3,17,128]{2,1,0:T(8,128)S(1)} collective-permute-done((f32[3,17,128]{2,1,0:T(8,128)S(1)}, f32[3,17,128]{2,1,0:T(8,128)S(1)}, u32[]{:S(2)}, u32[]{:S(2)}) %collective-permute-start.1) | collective-permute-done | bytes 26144 | tf_op jit(solution)/shard_map/ppermute | solution.py:162
  48.7 3.2 %collective-permute-done.2 = f32[3,17,128]{2,1,0:T(8,128)S(1)} collective-permute-done((f32[3,17,128]{2,1,0:T(8,128)S(1)}, f32[3,17,128]{2,1,0:T(8,128)S(1)}, u32[]{:S(2)}, u32[]{:S(2)}) %collective-permute-start.2) | collective-permute-done | bytes 26144 | tf_op jit(solution)/shard_map/ppermute | solution.py:162
  54.7 3.5 %all-to-all-start.1 = ((f32[4,12,2048]{2,1,0:T(8,128)}), f32[4,12,2048]{2,1,0:T(8,128)S(1)}, u32[]{:S(2)}, u32[]{:S(2)}) async-start(f32[4,12,2048]{2,1,0:T(8,128)} %broadcast_in_dim.89), calls=%async_computation.1 | async-start | bytes 1048576 | tf_op jit(solution)/shard_map/all_to_all | solution.py:57
  58.5 8.5 %all-to-all-done.1 = f32[4,12,2048]{2,1,0:T(8,128)S(1)} async-done(((f32[4,12,2048]{2,1,0:T(8,128)}), f32[4,12,2048]{2,1,0:T(8,128)S(1)}, u32[]{:S(2)}, u32[]{:S(2)}) %all-to-all-start.1) | async-done | bytes 393248 | tf_op jit(solution)/shard_map/all_to_all | solution.py:57
  69.6 13.3 %all_to_all.43 = bf16[8,2,9216]{2,1,0:T(2,128)(2,1)S(1)} all-to-all(bf16[8,2,9216]{2,1,0:T(2,128)(2,1)S(1)} %reshape.432), channel_id=1, replica_groups=mesh['req'=8,'tp'=4] {'req'}, dimensions={0} | all-to-all | bytes 589824 | tf_op jit(solution)/shard_map/all_to_all | solution.py:246
  83.8 1.9 %fusion.13 = f32[48,352]{1,0:T(8,128)S(1)} fusion(bf16[48,2048]{1,0:T(8,128)(2,1)S(1)} %reshape.387, bf16[1,2048,352]{1,2,0:T(8,128)(2,1)} %param.31), kind=kOutput, calls=%fused_computation.20 | convolution fusion | flops 69206016 | bytes 1705984 | tf_op jit(solution)/shard_map/dot_general | solution.py:250
  85.7 2.9 %convert_bitcast_fusion = (bf16[1,4,48,512]{3,2,1,0:T(8,128)(2,1)S(1)}, bf16[1,4,48,512]{3,2,1,0:T(8,128)(2,1)S(1)}) fusion(bf16[44,4,8,512]{3,2,1,0:T(8,128)(2,1)} %bitcast.203, bf16[48,2048]{1,0:T(8,128)(2,1)S(1)} %reshape.387, bf16[1,2048,352]{1,2,0:T(8,128)(2,1)} %param.32, f32[48,352]{1,0:T(8,128)S(1)} %fusion.13), kind=kOutput, calls=%fused_computation.86 | convolution fusion | flops 138906624 | bytes 3540992 | tf_op jit(solution)/shard_map/dot_general | solution.py:253
  92.4 5.0 %maximum_bitcast_fusion = bf16[4,1,184320]{2,0,1:T(4,128)(2,1)} fusion(bf16[4,24576]{1,0:T(4,128)(2,1)S(1)} %bitcast.209, bf16[4,24576]{1,0:T(4,128)(2,1)S(1)} %bitcast.208, bf16[184320]{0:T(1024)(128)(2,1)S(1)} %pad.4.clone), kind=kLoop, calls=%fused_computation.14 | loop fusion | flops 4423680 | bytes 2236416 | tf_op jit(solution)/shard_map/all_to_all | solution.py:274
  97.4 4.7 %reduce.6 = bf16[4,184320]{1,0:T(4,128)(2,1)} reduce(bf16[4,1,184320]{2,0,1:T(4,128)(2,1)} %maximum_bitcast_fusion, bf16[]{:T(256)} %broadcast.325), dimensions={1}, to_apply=%copy.226.reduce_sub_computation | reduce | bytes 2949122 | tf_op jit(solution)/shard_map/all_to_all | solution.py:274
  102.1 4.0 %reshape.434 = bf16[4,2,92160]{2,1,0:T(2,128)(2,1)} reshape(bf16[4,184320]{1,0:T(4,128)(2,1)} %reduce.6) | data formatting | bytes 2949120
  106.1 23.4 %all_to_all.44 = bf16[4,2,92160]{2,1,0:T(2,128)(2,1)} all-to-all(bf16[4,2,92160]{2,1,0:T(2,128)(2,1)} %reshape.434), channel_id=1, replica_groups=mesh['req'=8,'tp'=4] {'tp'}, dimensions={0} | all-to-all | bytes 2949120 | tf_op jit(solution)/shard_map/all_to_all | solution.py:274
  129.5 4.4 %reshape.435 = bf16[4,1,184320]{2,1,0:T(2,128)(2,1)} reshape(bf16[4,2,92160]{2,1,0:T(2,128)(2,1)} %all_to_all.44) | data formatting | bytes 2949120
  133.9 3.7 %copy.290 = f32[4,1,184320]{2,0,1:T(4,128)S(1)} copy(bf16[4,1,184320]{2,1,0:T(2,128)(2,1)} %reshape.435) | data formatting | bytes 4423680
  137.9 5.6 %slice_reduce_fusion = f32[135168]{0:T(1024)S(1)} fusion(f32[4,184320]{1,0:T(4,128)S(1)} %bitcast.202), kind=kLoop, calls=%fused_computation.13 | loop fusion | flops 405504 | bytes 2703360 | tf_op jit(solution)/shard_map/reduce_sum | solution.py:279
  146.1 3.4 %all-to-all-start.4 = ((f32[8,1,9216]{2,1,0:T(1,128)}), f32[8,1,9216]{2,1,0:T(1,128)S(1)}, u32[]{:S(2)}, u32[]{:S(2)}) async-start(f32[8,1,9216]{2,1,0:T(1,128)} %all_to_all.35), calls=%async_computation.4 | async-start | bytes 589824 | tf_op jit(solution)/shard_map/all_to_all | solution.py:292
  150.1 9.3 %all-to-all-done.4 = f32[8,1,9216]{2,1,0:T(1,128)S(1)} async-done(((f32[8,1,9216]{2,1,0:T(1,128)}), f32[8,1,9216]{2,1,0:T(1,128)S(1)}, u32[]{:S(2)}, u32[]{:S(2)}) %all-to-all-start.4) | async-done | bytes 294944 | tf_op jit(solution)/shard_map/all_to_all | solution.py:292
  (146 shorter events, 25.7 us)
Async XLA Ops:
  0.0 53.5 %copy-start = (bf16[512,2048]{1,0:T(8,128)(2,1)S(1)}, bf16[512,2048]{1,0:T(8,128)(2,1)}, u32[]{:S(2)}) copy-start(bf16[512,2048]{1,0:T(8,128)(2,1)} %param.23) | copy-start | bytes 6291460
  3.3 12.2 %copy-start.4 = (s32[3,4,4]{2,1,0:T(4,128)S(1)}, s32[3,4,4]{2,1,0:T(4,128)}, u32[]{:S(2)}) copy-start(s32[3,4,4]{2,1,0:T(4,128)} %param.29) | copy-start | bytes 580
  3.3 12.3 %copy-start.3 = (s32[24,37]{1,0:T(8,128)S(1)}, s32[24,37]{1,0:T(8,128)}, u32[]{:S(2)}) copy-start(s32[24,37]{1,0:T(8,128)} %param.26) | copy-start | bytes 10660
  3.3 12.6 %copy-start.1 = (s32[24]{0:T(128)S(1)}, s32[24]{0:T(128)}, u32[]{:S(2)}) copy-start(s32[24]{0:T(128)} %param.27) | copy-start | bytes 292
  8.1 14.4 %all-to-all-start = ((bf16[8,3,4,4,128]{4,3,2,1,0:T(4,128)(2,1)}), bf16[8,3,4,4,128]{4,3,2,1,0:T(4,128)(2,1)S(1)}, u32[]{:S(2)}, u32[]{:S(2)}) async-start(bf16[8,3,4,4,128]{4,3,2,1,0:T(4,128)(2,1)} %broadcast_in_dim.79), calls=%async_computation | async-start | bytes 196608 | tf_op jit(solution)/shard_map/all_to_all | solution.py:57
  35.0 8.0 %collective-permute-start = (f32[3,17,128]{2,1,0:T(8,128)S(1)}, f32[3,17,128]{2,1,0:T(8,128)S(1)}, u32[]{:S(2)}, u32[]{:S(2)}) collective-permute-start(f32[3,17,128]{2,1,0:T(8,128)S(1)} %get-tuple-element.26), channel_id=1, source_target_pairs={{0,4},{4,0},{8,12},{12,8},{16,20},{20,16},{24,28},{28,24},{1,5},{5... | collective-permute-start | bytes 78344 | tf_op jit(solution)/shard_map/ppermute | solution.py:162
  35.4 16.5 %collective-permute-start.6 = (f32[3,17,128]{2,1,0:T(8,128)S(1)}, f32[3,17,128]{2,1,0:T(8,128)S(1)}, u32[]{:S(2)}, u32[]{:S(2)}) collective-permute-start(f32[3,17,128]{2,1,0:T(8,128)S(1)} %get-tuple-element.20), channel_id=1, source_target_pairs={{0,28},{4,24},{8,20},{12,16},{16,12},{20,8},{24,4},{28,0},{1,29},{... | collective-permute-start | bytes 78344 | tf_op jit(solution)/shard_map/ppermute | solution.py:162
  37.1 14.8 %collective-permute-start.5 = (f32[3,17,128]{2,1,0:T(8,128)S(1)}, f32[3,17,128]{2,1,0:T(8,128)S(1)}, u32[]{:S(2)}, u32[]{:S(2)}) collective-permute-start(f32[3,17,128]{2,1,0:T(8,128)S(1)} %get-tuple-element.21), channel_id=1, source_target_pairs={{0,24},{4,28},{8,16},{12,20},{16,8},{20,12},{24,0},{28,4},{1,25},{... | collective-permute-start | bytes 78344 | tf_op jit(solution)/shard_map/ppermute | solution.py:162
  40.4 11.5 %collective-permute-start.4 = (f32[3,17,128]{2,1,0:T(8,128)S(1)}, f32[3,17,128]{2,1,0:T(8,128)S(1)}, u32[]{:S(2)}, u32[]{:S(2)}) collective-permute-start(f32[3,17,128]{2,1,0:T(8,128)S(1)} %get-tuple-element.22), channel_id=1, source_target_pairs={{0,20},{4,16},{8,28},{12,24},{16,4},{20,0},{24,12},{28,8},{1,21},{... | collective-permute-start | bytes 78344 | tf_op jit(solution)/shard_map/ppermute | solution.py:162
  40.4 11.5 %collective-permute-start.3 = (f32[3,17,128]{2,1,0:T(8,128)S(1)}, f32[3,17,128]{2,1,0:T(8,128)S(1)}, u32[]{:S(2)}, u32[]{:S(2)}) collective-permute-start(f32[3,17,128]{2,1,0:T(8,128)S(1)} %get-tuple-element.23), channel_id=1, source_target_pairs={{0,16},{4,20},{8,24},{12,28},{16,0},{20,4},{24,8},{28,12},{1,17},{... | collective-permute-start | bytes 78344 | tf_op jit(solution)/shard_map/ppermute | solution.py:162
  43.1 4.0 %collective-permute-start.1 = (f32[3,17,128]{2,1,0:T(8,128)S(1)}, f32[3,17,128]{2,1,0:T(8,128)S(1)}, u32[]{:S(2)}, u32[]{:S(2)}) collective-permute-start(f32[3,17,128]{2,1,0:T(8,128)S(1)} %get-tuple-element.25), channel_id=1, source_target_pairs={{0,8},{4,12},{8,0},{12,4},{16,24},{20,28},{24,16},{28,20},{1,9},{5... | collective-permute-start | bytes 78344 | tf_op jit(solution)/shard_map/ppermute | solution.py:162
  47.0 4.9 %collective-permute-start.2 = (f32[3,17,128]{2,1,0:T(8,128)S(1)}, f32[3,17,128]{2,1,0:T(8,128)S(1)}, u32[]{:S(2)}, u32[]{:S(2)}) collective-permute-start(f32[3,17,128]{2,1,0:T(8,128)S(1)} %get-tuple-element.24), channel_id=1, source_target_pairs={{0,12},{4,8},{8,4},{12,0},{16,28},{20,24},{24,20},{28,16},{1,13},{... | collective-permute-start | bytes 78344 | tf_op jit(solution)/shard_map/ppermute | solution.py:162
  51.9 6.3 %copy-start.2 = (bf16[3,4,2048]{2,1,0:T(4,128)(2,1)S(1)}, bf16[3,4,2048]{2,1,0:T(4,128)(2,1)}, u32[]{:S(2)}) copy-start(bf16[3,4,2048]{2,1,0:T(4,128)(2,1)} %param.19) | copy-start | bytes 147460
  52.0 6.3 %copy-start.6 = (bf16[2048]{0:T(1024)(128)(2,1)S(1)}, bf16[2048]{0:T(1024)(128)(2,1)}, u32[]{:S(2)}) copy-start(bf16[2048]{0:T(1024)(128)(2,1)} %param.28) | copy-start | bytes 12292
  54.7 12.3 %all-to-all-start.1 = ((f32[4,12,2048]{2,1,0:T(8,128)}), f32[4,12,2048]{2,1,0:T(8,128)S(1)}, u32[]{:S(2)}, u32[]{:S(2)}) async-start(f32[4,12,2048]{2,1,0:T(8,128)} %broadcast_in_dim.89), calls=%async_computation.1 | async-start | bytes 1048576 | tf_op jit(solution)/shard_map/all_to_all | solution.py:57
  143.5 6.1 %copy-start.5 = (f32[3,4,4]{2,1,0:T(4,128)S(1)}, f32[3,4,4]{2,1,0:T(4,128)}, u32[]{:S(2)}) copy-start(f32[3,4,4]{2,1,0:T(4,128)} %param.30) | copy-start | bytes 580
  143.5 6.1 %copy-start.7 = (bf16[2048]{0:T(1024)(128)(2,1)S(1)}, bf16[2048]{0:T(1024)(128)(2,1)}, u32[]{:S(2)}) copy-start(bf16[2048]{0:T(1024)(128)(2,1)} %param.37) | copy-start | bytes 12292
  146.1 13.3 %all-to-all-start.4 = ((f32[8,1,9216]{2,1,0:T(1,128)}), f32[8,1,9216]{2,1,0:T(1,128)S(1)}, u32[]{:S(2)}, u32[]{:S(2)}) async-start(f32[8,1,9216]{2,1,0:T(1,128)} %all_to_all.35), calls=%async_computation.4 | async-start | bytes 589824 | tf_op jit(solution)/shard_map/all_to_all | solution.py:292
